TPU v7x, 128 devices: a whole 4x4x4 slice. The times are simulated.
128 devices in a mesh: row: 8 (over x, y_hi), col: 16 (over y_lo, z, core).
Axes of the slice: x: 4, y: 4 (y_hi: 2, y_lo: 2; y = y_hi * 2 + y_lo), z: 4, core: 2. Of those that a mesh axis runs over, the one named last changes fastest.
Arguments:
- inputs: bfloat16 [8192, 4096], P('row', 'col'), may hold values from -5 to 5
- norm_gain: float32 [4096], replicated, may hold values from 0.25 to 1.75
- query_train: float32 [4096, 4096], P(('row', 'col')), as said below
- key_train: float32 [4096, 4096], P(('row', 'col')), as said below
- value_train: float32 [4096, 4096], P(('row', 'col')), may hold values from -0.09375 to 0.09375
- out_train: float32 [4096, 2048], P(None, ('row', 'col')), may hold values from -0.09375 to 0.09375
- adapter_down: bfloat16 [4096, 128], replicated, may hold values from -0.09375 to 0.09375
- adapter_up: bfloat16 [128, 3, 32, 128], P(None, None, 'col'), may hold values from -0.5 to 0.5
- lengths: int32 [8, 7], P('row'), may hold values from 1 to 512, 1024 in all within a row
Outputs:
- mixed: bfloat16 [8192, 2048], P(('row', 'col'))
Inputs may be any that keep to these rules, and one draw needn't show every extreme that they name: In each token group the 7 lengths sum to 1024; the longest is 512. `query_train`: entries are of order 1 / sqrt(4096) and at most 32 / sqrt(4096) in magnitude. `key_train`: entries are of order 1 / sqrt(4096) and at most 32 / sqrt(4096) in magnitude.
All inputs are finite; a program needn't handle non-finite values.
Results may differ from a plain program's by a relative error of at most 0.018.
Values may be sent and summed in bfloat16 or wider, within the bound.
No kernel may reach another device: no remote copies, remote signals or barrier semaphores. Data moves between devices by JAX's collectives and lax.ppermute only.
A program may use at most 128 MiB of HBM per device.

v0:
```python
import math

import jax
import jax.numpy as jnp
from jax import lax
from jax.sharding import PartitionSpec as P

HEADS = 32
HS = 128


def normalize(whole, norm_gain):
    floats = whole.astype(jnp.float32)
    mean_square = jnp.mean(floats * floats, axis=1, keepdims=True)
    return (floats * lax.rsqrt(mean_square + 1e-05) * norm_gain).astype(jnp.bfloat16)


def segment_of(lengths_row, tok_count):
    position = jnp.arange(tok_count, dtype=jnp.int32)
    prompt_ends = jnp.cumsum(lengths_row)
    return jnp.sum((position[:, None] >= prompt_ends[None, :]).astype(jnp.int32), axis=1)


def attend(queries, keys_all, values_all, segment):
    tok_count = queries.shape[0]
    block_rows = min(512, tok_count)
    factor = 1.0 / math.sqrt(queries.shape[2])
    key_pos = jnp.arange(tok_count, dtype=jnp.int32)

    def one_block(first):
        query_blk = lax.dynamic_slice_in_dim(queries, first, block_rows, 0)
        query_pos = first + jnp.arange(block_rows, dtype=jnp.int32)
        query_seg = lax.dynamic_slice_in_dim(segment, first, block_rows, 0)
        scores = (
            jnp.einsum("qhd,khd->hqk", query_blk, keys_all, preferred_element_type=jnp.float32)
            * factor
        )
        allowed = (query_seg[:, None] == segment[None, :]) & (
            key_pos[None, :] <= query_pos[:, None]
        )
        scores = jnp.where(allowed[None], scores, -1e30)
        highest = jnp.max(scores, axis=2, keepdims=True)
        exponent = jnp.exp(scores - highest)
        weights = (exponent / jnp.sum(exponent, axis=2, keepdims=True)).astype(jnp.bfloat16)
        return jnp.einsum(
            "hqk,khd->qhd", weights, values_all, preferred_element_type=jnp.float32
        ).astype(jnp.bfloat16)

    starts = jnp.arange(tok_count // block_rows, dtype=jnp.int32) * block_rows
    blocks = lax.map(one_block, starts)
    return blocks.reshape(tok_count, queries.shape[1] * queries.shape[2])


def on_device(
    inputs,
    norm_gain,
    query_train,
    key_train,
    value_train,
    out_train,
    adapter_down,
    adapter_up,
    lengths,
):
    col_count = lax.axis_size("col")
    whole = lax.all_gather(inputs, "col", axis=1, tiled=True)
    normed = normalize(whole, norm_gain)
    tok_count = normed.shape[0]
    adapted = jnp.dot(normed, adapter_down, preferred_element_type=jnp.float32).astype(jnp.bfloat16)
    local_rows = query_train.shape[0]
    head_local = HEADS // col_count
    merged_width = 3 * head_local * HS
    query_half = query_train.astype(jnp.bfloat16).reshape(local_rows, HEADS, HS)
    key_half = key_train.astype(jnp.bfloat16).reshape(local_rows, HEADS, HS)
    value_half = value_train.astype(jnp.bfloat16).reshape(local_rows, HEADS, HS)
    moved = (
        lax.all_to_all(query_half, "col", split_axis=1, concat_axis=0, tiled=True),
        lax.all_to_all(key_half, "col", split_axis=1, concat_axis=0, tiled=True),
        lax.all_to_all(value_half, "col", split_axis=1, concat_axis=0, tiled=True),
    )
    merged = jnp.stack(moved, axis=1).reshape(moved[0].shape[0], merged_width)
    product = jnp.dot(
        normed,
        lax.all_gather(merged, "row", axis=0, tiled=True),
        preferred_element_type=jnp.float32,
    )
    up_columns = adapter_up.reshape(adapter_up.shape[0], merged_width)
    joined = (product + jnp.dot(adapted, up_columns, preferred_element_type=jnp.float32)).astype(
        jnp.bfloat16
    )
    joined = joined.reshape(tok_count, 3, head_local, HS)
    segment = segment_of(lengths[0], tok_count)
    attended = attend(joined[:, 0], joined[:, 1], joined[:, 2], segment)
    out_local = out_train.astype(jnp.bfloat16)
    out_block = lax.all_to_all(out_local, "col", split_axis=0, concat_axis=1, tiled=True)
    partial_out = jnp.dot(
        attended,
        lax.all_gather(out_block, "row", axis=1, tiled=True),
        preferred_element_type=jnp.float32,
    )
    mixed = lax.psum_scatter(
        partial_out.astype(jnp.bfloat16), "col", scatter_dimension=0, tiled=True
    )
    return mixed


def solution(mesh):
    in_specs = (
        P("row", "col"),
        P(),
        P(("row", "col"), None),
        P(("row", "col"), None),
        P(("row", "col"), None),
        P(None, ("row", "col")),
        P(),
        P(None, None, "col", None),
        P("row", None),
    )
    out_specs = P(("row", "col"), None)
    return jax.shard_map(
        on_device, mesh=mesh, in_specs=in_specs, out_specs=out_specs, check_vma=False
    )
```

profile of v0, /device:TPU:0, one launch (start us, length us, event | category | flops | bytes accessed | tf_op | source)
XLA Modules:
  0.0 309.3 jit_solution(3217360996030934088)
XLA Ops:
  6.5 0.7 all-gather.4.cloned.1.call-update
  7.3 1.8 copy_bitcast_fusion
  9.0 6.5 %all-to-all-start.2 = ((bf16[32,32,128]{2,0,1:T(8,128)(2,1)}), bf16[32,32,128]{2,0,1:T(8,128)(2,1)S(1)}, u32[]{:S(2)}, u32[]{:S(2)}) async-start(bf16[32,32,128]{2,0,1:T(8,128)(2,1)} %copy_bitcast_fusion), calls=%async_computation.2 | async-start | bytes 524288 | tf_op jit(solution)/shard_map/all_to_all | solution.py:79
  15.6 1.8 copy_bitcast_fusion.2
  17.4 6.2 %all-to-all-done.2 = bf16[32,32,128]{2,0,1:T(8,128)(2,1)S(1)} async-done(((bf16[32,32,128]{2,0,1:T(8,128)(2,1)}), bf16[32,32,128]{2,0,1:T(8,128)(2,1)S(1)}, u32[]{:S(2)}, u32[]{:S(2)}) %all-to-all-start.2) | async-done | bytes 262176 | tf_op jit(solution)/shard_map/all_to_all | solution.py:79
  23.6 3.5 %all-to-all-start = ((bf16[32,32,128]{2,0,1:T(8,128)(2,1)}), bf16[32,32,128]{2,0,1:T(8,128)(2,1)S(1)}, u32[]{:S(2)}, u32[]{:S(2)}) async-start(bf16[32,32,128]{2,0,1:T(8,128)(2,1)} %copy_bitcast_fusion.2), calls=%async_computation | async-start | bytes 524288 | tf_op jit(solution)/shard_map/all_to_all | solution.py:77
  27.2 1.8 copy_bitcast_fusion.1
  28.9 9.1 %all-to-all-done = bf16[32,32,128]{2,0,1:T(8,128)(2,1)S(1)} async-done(((bf16[32,32,128]{2,0,1:T(8,128)(2,1)}), bf16[32,32,128]{2,0,1:T(8,128)(2,1)S(1)}, u32[]{:S(2)}, u32[]{:S(2)}) %all-to-all-start) | async-done | bytes 262176 | tf_op jit(solution)/shard_map/all_to_all | solution.py:77
  38.0 3.5 %all-to-all-start.1 = ((bf16[32,32,128]{2,0,1:T(8,128)(2,1)}), bf16[32,32,128]{2,0,1:T(8,128)(2,1)S(1)}, u32[]{:S(2)}, u32[]{:S(2)}) async-start(bf16[32,32,128]{2,0,1:T(8,128)(2,1)} %copy_bitcast_fusion.1), calls=%async_computation.1 | async-start | bytes 524288 | tf_op jit(solution)/shard_map/all_to_all | solution.py:78
  41.7 9.8 %all-to-all-done.1 = bf16[32,32,128]{2,0,1:T(8,128)(2,1)S(1)} async-done(((bf16[32,32,128]{2,0,1:T(8,128)(2,1)}), bf16[32,32,128]{2,0,1:T(8,128)(2,1)S(1)}, u32[]{:S(2)}, u32[]{:S(2)}) %all-to-all-start.1) | async-done | bytes 262176 | tf_op jit(solution)/shard_map/all_to_all | solution.py:78
  51.5 0.1 pad_maximum_fusion
  51.6 1.2 copy.56
  52.8 0.7 copy.81
  53.4 3.5 %all-to-all-start.3 = ((bf16[16,256,16]{1,2,0:T(8,128)(2,1)}), bf16[16,256,16]{1,2,0:T(8,128)(2,1)S(1)}, u32[]{:S(2)}, u32[]{:S(2)}) async-start(bf16[16,256,16]{1,2,0:T(8,128)(2,1)} %bitcast.57), calls=%async_computation.3 | async-start | bytes 262144 | tf_op jit(solution)/shard_map/all_to_all | solution.py:95
  57.0 0.0 all-gather.8.cloned.1.call-start
  57.0 0.1 reshape.128
  57.2 0.2 reduce-window.8
  57.3 0.1 convert_reduce_fusion
  57.4 7.9 %all-to-all-done.3 = bf16[16,256,16]{1,2,0:T(8,128)(2,1)S(1)} async-done(((bf16[16,256,16]{1,2,0:T(8,128)(2,1)}), bf16[16,256,16]{1,2,0:T(8,128)(2,1)S(1)}, u32[]{:S(2)}, u32[]{:S(2)}) %all-to-all-start.3) | async-done | bytes 131104 | tf_op jit(solution)/shard_map/all_to_all | solution.py:95
  65.4 0.7 copy-done.1
  66.1 0.0 reduce-scatter.2.cloned.1.call-start
  66.1 14.7 %all-gather.4.cloned.1.call-done = bf16[1024,4096]{1,0:T(8,128)(2,1)} async-done(((bf16[1024,256]{1,0:T(8,128)(2,1)}), bf16[1024,4096]{1,0:T(8,128)(2,1)}) %all-gather.4.cloned.1.call-update) | async-done | bytes 8388624 | tf_op jit(solution)/shard_map/all_gather | solution.py:66
  80.8 5.1 %fusion.26 = f32[1024]{0:T(1024)S(1)} fusion(bf16[1024,4096]{1,0:T(8,128)(2,1)} %all-gather.4.cloned.1.call-done), kind=kLoop, calls=%fused_computation.26 | loop fusion | flops 12581888 | bytes 8392704 | tf_op jit(solution)/shard_map/reduce_sum | solution.py:14
  85.9 97.2 %all-gather.6.cloned.1.call-done = bf16[4096,768]{0,1:T(8,128)(2,1)} async-done(((bf16[512,768]{0,1:T(8,128)(2,1)}), bf16[4096,768]{0,1:T(8,128)(2,1)}) %all-gather.6.cloned.1.call-update) | async-done | bytes 6291472 | tf_op jit(solution)/shard_map/all_gather | solution.py:84
  183.2 12.6 %fusion.31 = f32[1024,768]{0,1:T(8,128)} fusion(bf16[4096,768]{0,1:T(8,128)(2,1)} %all-gather.6.cloned.1.call-done, bf16[1024,4096]{1,0:T(8,128)(2,1)} %all-gather.4.cloned.1.call-done, f32[4096]{0:T(1024)S(1)} %copy-done.4, f32[1024]{0:T(1024)S(1)} %add_rsqrt_fusion), kind=kOutput, calls=%fused_computation.32 | convolution fusion | flops 6459228160 | bytes 17846272 | tf_op jit(solution)/shard_map/dot_general | solution.py:82
  195.8 9.0 %add_convert_fusion = bf16[1024,768]{0,1:T(8,128)(2,1)} fusion(f32[1024,768]{0,1:T(8,128)} %fusion.31, bf16[128,768]{1,0:T(8,128)(2,1)S(1)} %reshape.128, bf16[4096,128]{1,0:T(8,128)(2,1)S(1)} %copy-done, bf16[1024,4096]{1,0:T(8,128)(2,1)} %all-gather.4.cloned.1.call-done, f32[4096]{0:T(1024)S(1)} %copy-done.4, f32[1024]{0:T(1024)S(1)} %add_rsqrt_fusion), kind=kOutput, calls=%fused_computation.30 | convolution fusion | flops 1293549568 | bytes 14372864 | tf_op jit(solution)/shard_map/dot_general | solution.py:88
  204.8 1.5 fusion.45
  206.3 1.0 copy.64
  207.3 0.3 copy.65
  207.6 0.3 copy.66
  207.9 23.4 %while.11 = (s32[]{:T(128)}, bf16[2,512,2,128]{3,2,1,0:T(2,128)(2,1)S(1)}, s32[2]{0:T(128)S(1)}, s32[1024]{0:T(1024)S(1)}, bf16[1024,2,128]{2,0,1:T(8,128)(2,1)}...) while((s32[]{:T(128)}, ...), condition=%wide.region_6.7_spmd.clone, body=%wide.region_3.6_spmd.clone.sunk | while | flops 544867840 | bytes 11557027 | solution.py:50
  207.9 0.7 dynamic_slice.29
  210.4 0.1 dynamic_slice.30
  210.5 0.6 iota_add_fusion.2
  211.1 0.6 fusion.62
  211.7 4.6 %fusion.63 = (f32[2,512]{1,0:T(2,128)S(1)}, f32[2,512,1024]{2,1,0:T(8,128)}) fusion(pred[512,1024]{1,0:T(8,128)(4,1)S(1)} %fusion.62, bf16[1024,2,128]{2,0,1:T(8,128)(2,1)S(1)} %get-tuple-element.155, bf16[1024,2,128]{2,0,1:T(8,128)(2,1)} %get-tuple-element.154, s32[]{:T(128)S(6)} %select_n.23), kind=kOutput, calls=%fused_computation.48.clone.1 | convolution fusion | flops 272630784 | bytes 5509124 | tf_op jit(solution)/shard_map/while/body/eval_jaxpr/sub | solution.py:43
  216.3 3.0 fusion.64
  219.3 0.3 copy_dynamic-update-slice_fusion.2
  219.6 0.7 dynamic_slice.29
  222.1 0.1 dynamic_slice.30
  222.2 0.6 iota_add_fusion.2
  222.8 0.6 fusion.62
  223.4 4.6 %fusion.63 = (f32[2,512]{1,0:T(2,128)S(1)}, f32[2,512,1024]{2,1,0:T(8,128)}) fusion(pred[512,1024]{1,0:T(8,128)(4,1)S(1)} %fusion.62, bf16[1024,2,128]{2,0,1:T(8,128)(2,1)S(1)} %get-tuple-element.155, bf16[1024,2,128]{2,0,1:T(8,128)(2,1)} %get-tuple-element.154, s32[]{:T(128)S(6)} %select_n.23), kind=kOutput, calls=%fused_computation.48.clone.1 | convolution fusion | flops 272630784 | bytes 5509124 | tf_op jit(solution)/shard_map/while/body/eval_jaxpr/sub | solution.py:43
  228.0 3.0 fusion.64
  231.0 0.3 copy_dynamic-update-slice_fusion.2
  231.3 0.1 all-gather.8.cloned.1.call-done
  231.4 4.5 %convolution_convert_fusion = bf16[1024,2048]{1,0:T(8,128)(2,1)} fusion(bf16[256,2048]{0,1:T(8,128)(2,1)} %all-gather.8.cloned.1.call-done, bf16[128,8,2,128]{3,2,1,0:T(2,128)(2,1)S(1)} %bitcast.67), kind=kOutput, calls=%fused_computation.29 | convolution fusion | flops 1075838976 | bytes 5767168 | tf_op jit(solution)/shard_map/dot_general | solution.py:96
  235.9 66.8 %reduce-scatter.2.cloned.1.call-done = bf16[64,2048]{1,0:T(8,128)(2,1)} async-done(((bf16[1024,2048]{1,0:T(8,128)(2,1)}), bf16[64,2048]{1,0:T(8,128)(2,1)}) %reduce-scatter.2.cloned.1.call-update) | async-done | bytes 262160 | tf_op jit(solution)/shard_map/reduce_scatter | solution.py:101
  (23 shorter events, 0.2 us)
Async XLA Ops:
  6.5 189.2 %copy-start = (bf16[4096,128]{1,0:T(8,128)(2,1)S(1)}, bf16[4096,128]{1,0:T(8,128)(2,1)}, u32[]{:S(2)}) copy-start(bf16[4096,128]{1,0:T(8,128)(2,1)} %param.17) | copy-start | bytes 3145732
  6.5 74.3 %all-gather.4.cloned.1.call-start = ((), (), s32[]{:S(2)}) async-start(), calls=%async_computation.5 | async-start | bytes 8912896 | tf_op jit(solution)/shard_map/all_gather | solution.py:66
  9.0 14.6 %all-to-all-start.2 = ((bf16[32,32,128]{2,0,1:T(8,128)(2,1)}), bf16[32,32,128]{2,0,1:T(8,128)(2,1)S(1)}, u32[]{:S(2)}, u32[]{:S(2)}) async-start(bf16[32,32,128]{2,0,1:T(8,128)(2,1)} %copy_bitcast_fusion), calls=%async_computation.2 | async-start | bytes 524288 | tf_op jit(solution)/shard_map/all_to_all | solution.py:79
  15.6 37.2 %copy-start.2 = (f32[4096,16]{0,1:T(8,128)S(1)}, f32[4096,16]{0,1:T(8,128)}, u32[]{:S(2)}) copy-start(f32[4096,16]{0,1:T(8,128)} %param.16) | copy-start | bytes 786436
  17.4 39.6 %copy-start.3 = (bf16[128,3,2,128]{3,2,1,0:T(2,128)(2,1)S(1)}, bf16[128,3,2,128]{3,2,1,0:T(2,128)(2,1)}, u32[]{:S(2)}) copy-start(bf16[128,3,2,128]{3,2,1,0:T(2,128)(2,1)} %param.18) | copy-start | bytes 589828
  23.6 14.4 %all-to-all-start = ((bf16[32,32,128]{2,0,1:T(8,128)(2,1)}), bf16[32,32,128]{2,0,1:T(8,128)(2,1)S(1)}, u32[]{:S(2)}, u32[]{:S(2)}) async-start(bf16[32,32,128]{2,0,1:T(8,128)(2,1)} %copy_bitcast_fusion.2), calls=%async_computation | async-start | bytes 524288 | tf_op jit(solution)/shard_map/all_to_all | solution.py:77
  27.1 30.0 %copy-start.5 = (s32[1,7]{1,0:T(1,128)S(1)}, s32[1,7]{1,0:T(1,128)}, u32[]{:S(2)}) copy-start(s32[1,7]{1,0:T(1,128)} %param.19) | copy-start | bytes 88
  38.0 13.4 %all-to-all-start.1 = ((bf16[32,32,128]{2,0,1:T(8,128)(2,1)}), bf16[32,32,128]{2,0,1:T(8,128)(2,1)S(1)}, u32[]{:S(2)}, u32[]{:S(2)}) async-start(bf16[32,32,128]{2,0,1:T(8,128)(2,1)} %copy_bitcast_fusion.1), calls=%async_computation.1 | async-start | bytes 524288 | tf_op jit(solution)/shard_map/all_to_all | solution.py:78
  41.6 141.6 %all-gather.6.cloned.1.call-start = ((), (), s32[]{:S(2)}) async-start(), calls=%async_computation.6 | async-start | bytes 7077888 | tf_op jit(solution)/shard_map/all_gather | solution.py:84
  53.4 11.9 %all-to-all-start.3 = ((bf16[16,256,16]{1,2,0:T(8,128)(2,1)}), bf16[16,256,16]{1,2,0:T(8,128)(2,1)S(1)}, u32[]{:S(2)}, u32[]{:S(2)}) async-start(bf16[16,256,16]{1,2,0:T(8,128)(2,1)} %bitcast.57), calls=%async_computation.3 | async-start | bytes 262144 | tf_op jit(solution)/shard_map/all_to_all | solution.py:95
  57.0 174.5 %all-gather.8.cloned.1.call-start = ((), (), s32[]{:S(2)}) async-start(), calls=%async_computation.7 | async-start | bytes 1179648 | tf_op jit(solution)/shard_map/all_gather | solution.py:98
  65.4 0.7 copy-start.1
  66.0 117.1 %copy-start.4 = (f32[4096]{0:T(1024)S(1)}, f32[4096]{0:T(1024)}, u32[]{:S(2)}) copy-start(f32[4096]{0:T(1024)} %param.12) | copy-start | bytes 49156
  66.1 236.7 %reduce-scatter.2.cloned.1.call-start = ((), (), s32[]{:S(2)}) async-start(), calls=%async_computation.8 | async-start | bytes 4456448 | tf_op jit(solution)/shard_map/reduce_scatter | solution.py:101
Sparse Core Ops, SparseCore 0:
  9.0 71.8 all-gather.3
  83.0 100.0 all-gather.5
  185.5 45.8 all-gather.7
  236.1 66.6 reduce-scatter.1
where the time goes:
time: 310 us; the launch traced here: 309 us
  waiting for transfers between devices  213 us (69%)
  matrix products  41.2 us (13%)
  starting transfers between devices  17.2 us (6%)
  other arithmetic  13.3 us (4%)
  between operations  13.3 us (4%)
  local copies, waits for them, and re-layouts  7.78 us (3%)
  loops' own time  3.82 us (1%)
    all_gather x1, waiting for transfers between devices, on_device(): lax.all_gather(merged, 'row', axis=0, tiled=True)  97.2 us
    reduce_scatter x1, waiting for transfers between devices, on_device(): lax.psum_scatter(partial_out.astype(jnp.bfloat16), 'col', scatter_dimensi...  66.8 us
    all_gather x1, waiting for transfers between devices, on_device(): whole = lax.all_gather(inputs, 'col', axis=1, tiled=True)  14.7 us
    dot_general x1, matrix products, on_device(): jnp.dot(normed, lax.all_gather(merged, 'row', axis=0, tiled=True), prefer...  12.6 us
    all_to_all x1, waiting for transfers between devices, on_device(): lax.all_to_all(key_half, 'col', split_axis=1, concat_axis=0, tiled=True)  9.77 us
    sub x2, matrix products, one_block(): exponent = jnp.exp(scores - highest)  9.25 us
    all_to_all x1, waiting for transfers between devices, on_device(): lax.all_to_all(query_half, 'col', split_axis=1, concat_axis=0, tiled=True)  9.07 us
    dot_general x1, matrix products, on_device(): jnp.dot(adapted, up_columns, preferred_element_type=jnp.float32)  9 us
  transfers between devices with their start and end apart: 8, of which 8 were waited for; matrix products, arithmetic and copies ran while one was open for 18% of the time, Pallas kernels for 0%

commit v1 on v0

--- a/solution.py
+++ b/solution.py
@@ -68,22 +68,19 @@
     tok_count = normed.shape[0]
     adapted = jnp.dot(normed, adapter_down, preferred_element_type=jnp.float32).astype(jnp.bfloat16)
     local_rows = query_train.shape[0]
+    row_count = lax.axis_size("row")
     head_local = HEADS // col_count
     merged_width = 3 * head_local * HS
-    query_half = query_train.astype(jnp.bfloat16).reshape(local_rows, HEADS, HS)
-    key_half = key_train.astype(jnp.bfloat16).reshape(local_rows, HEADS, HS)
-    value_half = value_train.astype(jnp.bfloat16).reshape(local_rows, HEADS, HS)
-    moved = (
-        lax.all_to_all(query_half, "col", split_axis=1, concat_axis=0, tiled=True),
-        lax.all_to_all(key_half, "col", split_axis=1, concat_axis=0, tiled=True),
-        lax.all_to_all(value_half, "col", split_axis=1, concat_axis=0, tiled=True),
+    trained = jnp.stack(
+        (query_train.astype(jnp.bfloat16), key_train.astype(jnp.bfloat16), value_train.astype(jnp.bfloat16)),
+        axis=1,
+    ).reshape(local_rows, 3, col_count, head_local * HS)
+    trained = jnp.transpose(trained, (2, 0, 1, 3)).reshape(col_count, local_rows, merged_width)
+    sent = jnp.broadcast_to(trained[None], (row_count,) + trained.shape).reshape(
+        row_count * col_count, local_rows, merged_width
     )
-    merged = jnp.stack(moved, axis=1).reshape(moved[0].shape[0], merged_width)
-    product = jnp.dot(
-        normed,
-        lax.all_gather(merged, "row", axis=0, tiled=True),
-        preferred_element_type=jnp.float32,
-    )
+    merged = lax.all_to_all(sent, ("row", "col"), 0, 0, tiled=True).reshape(-1, merged_width)
+    product = jnp.dot(normed, merged, preferred_element_type=jnp.float32)
     up_columns = adapter_up.reshape(adapter_up.shape[0], merged_width)
     joined = (product + jnp.dot(adapted, up_columns, preferred_element_type=jnp.float32)).astype(
         jnp.bfloat16
@@ -92,12 +89,14 @@
     segment = segment_of(lengths[0], tok_count)
     attended = attend(joined[:, 0], joined[:, 1], joined[:, 2], segment)
     out_local = out_train.astype(jnp.bfloat16)
-    out_block = lax.all_to_all(out_local, "col", split_axis=0, concat_axis=1, tiled=True)
-    partial_out = jnp.dot(
-        attended,
-        lax.all_gather(out_block, "row", axis=1, tiled=True),
-        preferred_element_type=jnp.float32,
+    out_cols = out_local.shape[1]
+    out_sent = out_local.reshape(col_count, head_local * HS, out_cols)
+    out_sent = jnp.broadcast_to(out_sent[None], (row_count,) + out_sent.shape).reshape(
+        row_count * col_count, head_local * HS, out_cols
     )
+    out_block = lax.all_to_all(out_sent, ("row", "col"), 0, 0, tiled=True)
+    out_block = jnp.transpose(out_block, (1, 0, 2)).reshape(head_local * HS, -1)
+    partial_out = jnp.dot(attended, out_block, preferred_element_type=jnp.float32)
     mixed = lax.psum_scatter(
         partial_out.astype(jnp.bfloat16), "col", scatter_dimension=0, tiled=True
     )

time: 310 us -> 290 us (0.935)
  waiting for transfers between devices: 213 us -> 184 us
  local copies, waits for them, and re-layouts: 7.78 us -> 16.3 us
    all_gather x1, waiting for transfers between devices: 14.7 us -> 115 us  [on_device(): whole = lax.all_gather(inputs, 'col', axis=1, tiled=True)]
    all_gather x2 -> x0, waiting for transfers between devices: 97.4 us -> none  [the longest x1 97.2 us: on_device(): lax.all_gather(merged, 'row', axis=0, tiled=True)]
    all_to_all x4 -> x2, waiting for transfers between devices: 32.9 us -> 0.01 us  [the longest x1 0.01 us: on_device(): out_block = lax.all_to_all(out_sent, ('row', 'col'), 0, 0, tiled=True)]
    broadcast_in_dim x0 -> x4, local copies, waits for them, and re-layouts: none -> 5.42 us  [the longest x2 4.31 us: on_device(): jnp.broadcast_to(trained[None], (row_count,) + trained.shape)]
    reshape x3 -> x0, other arithmetic: 5.41 us -> none  [the longest x1 1.85 us: on_device(): query_half = query_train.astype(jnp.bfloat16).reshape(local_rows, HEADS, HS)]
    all_to_all x4 -> x2, starting transfers between devices: 17.1 us -> 17.3 us  [the longest x1 11.6 us: on_device(): lax.all_to_all(sent, ('row', 'col'), 0, 0, tiled=True)]
  transfers between devices with their start and end apart: 8 -> 4, of which waited for: 8 -> 2; matrix products, arithmetic and copies ran while one was open for 18% -> 22% of each run, Pallas kernels for 0% -> 0%
where the time goes in v1:
time: 290 us; the launch traced here: 289 us
  waiting for transfers between devices  184 us (63%)
  matrix products  41.4 us (14%)
  starting transfers between devices  17.6 us (6%)
  local copies, waits for them, and re-layouts  16.3 us (6%)
  between operations  13.6 us (5%)
  other arithmetic  11.8 us (4%)
  loops' own time  3.86 us (1%)
    all_gather x1, waiting for transfers between devices, on_device(): whole = lax.all_gather(inputs, 'col', axis=1, tiled=True)  115 us
    reduce_scatter x1, waiting for transfers between devices, on_device(): lax.psum_scatter(partial_out.astype(jnp.bfloat16), 'col', scatter_dimensi...  69 us
    dot_general x1, matrix products, on_device(): product = jnp.dot(normed, merged, preferred_element_type=jnp.float32)  12.6 us
    all_to_all x1, starting transfers between devices, on_device(): lax.all_to_all(sent, ('row', 'col'), 0, 0, tiled=True)  11.6 us
    sub x2, matrix products, one_block(): exponent = jnp.exp(scores - highest)  9.51 us
    dot_general x1, matrix products, on_device(): jnp.dot(adapted, up_columns, preferred_element_type=jnp.float32)  9.04 us
    dot_general x2, matrix products, one_block(): jnp.einsum('hqk,khd->qhd', weights, values_all, preferred_element_type=jn...  6 us
  transfers between devices with their start and end apart: 4, of which 2 were waited for; matrix products, arithmetic and copies ran while one was open for 22% of the time, Pallas kernels for 0%

profile of v1, /device:TPU:0, one launch (start us, length us, event | category | flops | bytes accessed | tf_op | source)
XLA Modules:
  0.0 289.0 jit_solution(10989995483532322159)
XLA Ops:
  6.5 0.0 copy-start
  6.5 0.7 all-gather.2.cloned.1.call-update
  7.3 1.1 convert_element_type.44
  8.4 0.5 copy.24
  8.9 1.1 convert_element_type.43
  10.0 0.5 copy.23
  10.6 0.5 copy.22
  11.1 1.8 maximum_bitcast_fusion
  13.0 0.9 broadcast_in_dim.34
  13.9 3.4 %broadcast_in_dim.46 = bf16[8,16,32,768]{3,2,1,0:T(8,128)(2,1)} broadcast(bf16[16,32,768]{2,1,0:T(8,128)(2,1)S(1)} %broadcast_in_dim.34), dimensions={1,2,3} | broadcast | bytes 7077888 | tf_op jit(solution)/shard_map/broadcast_in_dim | solution.py:79
  17.3 11.6 %all-to-all-start = ((bf16[128,32,768]{2,1,0:T(8,128)(2,1)}), bf16[128,32,768]{2,1,0:T(8,128)(2,1)}, u32[]{:S(2)}, u32[]{:S(2)}) async-start(bf16[128,32,768]{2,1,0:T(8,128)(2,1)} %bitcast.55), calls=%async_computation | async-start | bytes 12582912 | tf_op jit(solution)/shard_map/all_to_all | solution.py:82
  29.0 0.2 reduce-window.8
  29.2 0.1 reshape.129
  29.3 0.1 convert_reduce_fusion
  29.4 0.0 copy-start.6
  29.4 114.8 %all-gather.2.cloned.1.call-done = bf16[1024,4096]{1,0:T(8,128)(2,1)} async-done(((bf16[1024,256]{1,0:T(8,128)(2,1)}), bf16[1024,4096]{1,0:T(8,128)(2,1)}) %all-gather.2.cloned.1.call-update) | async-done | bytes 8388624 | tf_op jit(solution)/shard_map/all_gather | solution.py:66
  144.2 5.1 %fusion.26 = f32[1024]{0:T(1024)S(1)} fusion(bf16[1024,4096]{1,0:T(8,128)(2,1)} %all-gather.2.cloned.1.call-done), kind=kLoop, calls=%fused_computation.26 | loop fusion | flops 12581888 | bytes 8392704 | tf_op jit(solution)/shard_map/reduce_sum | solution.py:14
  149.3 0.0 all-to-all-done
  149.3 1.1 broadcast_in_dim.48
  150.4 5.7 %all-to-all-start.1 = ((bf16[128,256,16]{1,2,0:T(8,128)(2,1)}), bf16[128,256,16]{1,2,0:T(8,128)(2,1)S(1)}, u32[]{:S(2)}, u32[]{:S(2)}) async-start(bf16[128,256,16]{1,2,0:T(8,128)(2,1)} %bitcast.9), calls=%async_computation.1 | async-start | bytes 2097152 | tf_op jit(solution)/shard_map/all_to_all | solution.py:97
  156.1 0.2 reduce-scatter.2.cloned.1.call-start
  156.3 12.6 %fusion.31 = f32[1024,768]{0,1:T(8,128)} fusion(bf16[4096,768]{1,0:T(8,128)(2,1)} %bitcast.4, bf16[1024,4096]{1,0:T(8,128)(2,1)} %all-gather.2.cloned.1.call-done, f32[4096]{0:T(1024)S(1)} %copy-done.6, f32[1024]{0:T(1024)S(1)} %add_rsqrt_fusion), kind=kOutput, calls=%fused_computation.32 | convolution fusion | flops 6459228160 | bytes 17846272 | tf_op jit(solution)/shard_map/dot_general | solution.py:83
  168.9 9.0 %add_convert_fusion = bf16[1024,768]{0,1:T(8,128)(2,1)} fusion(f32[1024,768]{0,1:T(8,128)} %fusion.31, bf16[128,768]{1,0:T(8,128)(2,1)S(1)} %reshape.129, bf16[4096,128]{1,0:T(8,128)(2,1)S(1)} %copy-done, bf16[1024,4096]{1,0:T(8,128)(2,1)} %all-gather.2.cloned.1.call-done, f32[4096]{0:T(1024)S(1)} %copy-done.6, f32[1024]{0:T(1024)S(1)} %add_rsqrt_fusion), kind=kOutput, calls=%fused_computation.30 | convolution fusion | flops 1293549568 | bytes 14372864 | tf_op jit(solution)/shard_map/dot_general | solution.py:85
  178.0 2.3 fusion.45
  180.3 2.0 copy.32
  182.3 1.0 copy.33
  183.4 0.3 copy.34
  183.6 25.3 %while.11 = (s32[]{:T(128)}, bf16[2,512,2,128]{3,2,1,0:T(2,128)(2,1)}, s32[2]{0:T(128)S(1)}, s32[1024]{0:T(1024)S(1)}, bf16[1024,2,128]{2,0,1:T(8,128)(2,1)}, /*...) while((s32[]{:T(128)}, ...), condition=%wide.region_6.7_spmd.clone, body=%wide.region_3.6_spmd.clone.sunk | while | flops 544867840 | bytes 15751395 | solution.py:50
  183.7 0.6 dynamic_slice.29
  184.3 0.6 iota_add_fusion.2
  186.8 0.1 dynamic_slice.30
  186.8 0.6 fusion.62
  187.4 4.8 %fusion.63 = (f32[2,512]{1,0:T(2,128)S(1)}, f32[2,512,1024]{2,1,0:T(8,128)}) fusion(pred[512,1024]{1,0:T(8,128)(4,1)S(1)} %fusion.62, bf16[1024,2,128]{2,0,1:T(8,128)(2,1)} %get-tuple-element.155, bf16[1024,2,128]{2,0,1:T(8,128)(2,1)} %get-tuple-element.154, s32[]{:T(128)S(6)} %select_n.23), kind=kOutput, calls=%fused_computation.42.clone.1 | convolution fusion | flops 272630784 | bytes 5509124 | tf_op jit(solution)/shard_map/while/body/eval_jaxpr/sub | solution.py:43
  192.2 3.0 %fusion.64 = bf16[1,512,2,128]{3,1,2,0:T(8,128)(2,1)S(1)} fusion(bf16[1024,2,128]{2,0,1:T(8,128)(2,1)S(1)} %get-tuple-element.156, f32[2,512,1024]{2,1,0:T(8,128)} %get-tuple-element.128, f32[2,512]{1,0:T(2,128)S(1)} %get-tuple-element.129), kind=kOutput, calls=%fused_computation.13.clone.1 | convolution fusion | flops 270663680 | bytes 4984832 | tf_op jit(solution)/shard_map/while/body/eval_jaxpr/hqk,khd->qhd/dot_general | solution.py:45
  195.2 0.3 copy_dynamic-update-slice_fusion.2
  195.5 0.8 copy-done.2
  196.3 0.6 dynamic_slice.29
  196.9 0.6 iota_add_fusion.2
  199.4 0.1 dynamic_slice.30
  199.5 0.6 fusion.62
  200.1 4.8 %fusion.63 = (f32[2,512]{1,0:T(2,128)S(1)}, f32[2,512,1024]{2,1,0:T(8,128)}) fusion(pred[512,1024]{1,0:T(8,128)(4,1)S(1)} %fusion.62, bf16[1024,2,128]{2,0,1:T(8,128)(2,1)} %get-tuple-element.155, bf16[1024,2,128]{2,0,1:T(8,128)(2,1)} %get-tuple-element.154, s32[]{:T(128)S(6)} %select_n.23), kind=kOutput, calls=%fused_computation.42.clone.1 | convolution fusion | flops 272630784 | bytes 5509124 | tf_op jit(solution)/shard_map/while/body/eval_jaxpr/sub | solution.py:43
  204.8 3.0 %fusion.64 = bf16[1,512,2,128]{3,1,2,0:T(8,128)(2,1)S(1)} fusion(bf16[1024,2,128]{2,0,1:T(8,128)(2,1)S(1)} %get-tuple-element.156, f32[2,512,1024]{2,1,0:T(8,128)} %get-tuple-element.128, f32[2,512]{1,0:T(2,128)S(1)} %get-tuple-element.129), kind=kOutput, calls=%fused_computation.13.clone.1 | convolution fusion | flops 270663680 | bytes 4984832 | tf_op jit(solution)/shard_map/while/body/eval_jaxpr/hqk,khd->qhd/dot_general | solution.py:45
  207.9 0.3 copy_dynamic-update-slice_fusion.2
  208.2 0.8 copy-done.2
  208.9 0.0 all-to-all-done.1
  209.0 4.3 %convolution_convert_fusion = bf16[1024,2048]{1,0:T(8,128)(2,1)} fusion(bf16[256,2048]{0,1:T(8,128)(2,1)S(1)} %bitcast.56, bf16[128,8,2,128]{3,2,1,0:T(2,128)(2,1)} %bitcast.57), kind=kOutput, calls=%fused_computation.29 | convolution fusion | flops 1075838976 | bytes 5767168 | tf_op jit(solution)/shard_map/dot_general | solution.py:99
  213.2 0.0 reduce-scatter.2.cloned.1.call-update
  213.3 69.0 %reduce-scatter.2.cloned.1.call-done = bf16[64,2048]{1,0:T(8,128)(2,1)} async-done(((bf16[1024,2048]{1,0:T(8,128)(2,1)}), bf16[64,2048]{1,0:T(8,128)(2,1)}) %reduce-scatter.2.cloned.1.call-update) | async-done | bytes 262160 | tf_op jit(solution)/shard_map/reduce_scatter | solution.py:100
  (26 shorter events, 0.2 us)
Async XLA Ops:
  6.5 162.4 %copy-start = (bf16[4096,128]{1,0:T(8,128)(2,1)S(1)}, bf16[4096,128]{1,0:T(8,128)(2,1)}, u32[]{:S(2)}) copy-start(bf16[4096,128]{1,0:T(8,128)(2,1)} %param.17) | copy-start | bytes 3145732
  6.5 4.0 %copy-start.3 = (f32[32,4096]{1,0:T(8,128)S(1)}, f32[32,4096]{1,0:T(8,128)}, u32[]{:S(2)}) copy-start(f32[32,4096]{1,0:T(8,128)} %param.13) | copy-start | bytes 1572868
  6.5 137.7 %all-gather.2.cloned.1.call-start = ((), (), s32[]{:S(2)}) async-start(), calls=%async_computation.3 | async-start | bytes 8912896 | tf_op jit(solution)/shard_map/all_gather | solution.py:66
  17.3 11.7 %copy-start.4 = (f32[4096,16]{0,1:T(8,128)S(1)}, f32[4096,16]{0,1:T(8,128)}, u32[]{:S(2)}) copy-start(f32[4096,16]{0,1:T(8,128)} %param.16) | copy-start | bytes 786436
  17.3 11.7 %copy-start.7 = (s32[1,7]{1,0:T(1,128)S(1)}, s32[1,7]{1,0:T(1,128)}, u32[]{:S(2)}) copy-start(s32[1,7]{1,0:T(1,128)} %param.19) | copy-start | bytes 88
  17.3 11.9 %copy-start.5 = (bf16[128,3,2,128]{3,2,1,0:T(2,128)(2,1)S(1)}, bf16[128,3,2,128]{3,2,1,0:T(2,128)(2,1)}, u32[]{:S(2)}) copy-start(bf16[128,3,2,128]{3,2,1,0:T(2,128)(2,1)} %param.18) | copy-start | bytes 589828
  17.3 132.0 %all-to-all-start = ((bf16[128,32,768]{2,1,0:T(8,128)(2,1)}), bf16[128,32,768]{2,1,0:T(8,128)(2,1)}, u32[]{:S(2)}, u32[]{:S(2)}) async-start(bf16[128,32,768]{2,1,0:T(8,128)(2,1)} %bitcast.55), calls=%async_computation | async-start | bytes 12582912 | tf_op jit(solution)/shard_map/all_to_all | solution.py:82
  29.4 126.9 %copy-start.6 = (f32[4096]{0:T(1024)S(1)}, f32[4096]{0:T(1024)}, u32[]{:S(2)}) copy-start(f32[4096]{0:T(1024)} %param.12) | copy-start | bytes 49156
  150.4 58.6 %all-to-all-start.1 = ((bf16[128,256,16]{1,2,0:T(8,128)(2,1)}), bf16[128,256,16]{1,2,0:T(8,128)(2,1)S(1)}, u32[]{:S(2)}, u32[]{:S(2)}) async-start(bf16[128,256,16]{1,2,0:T(8,128)(2,1)} %bitcast.9), calls=%async_computation.1 | async-start | bytes 2097152 | tf_op jit(solution)/shard_map/all_to_all | solution.py:97
  156.1 126.1 %reduce-scatter.2.cloned.1.call-start = ((), (), s32[]{:S(2)}) async-start(), calls=%async_computation.4 | async-start | bytes 4456448 | tf_op jit(solution)/shard_map/reduce_scatter | solution.py:100
  192.2 3.0 %copy-start.1 = (bf16[2,512,2,128]{3,2,1,0:T(2,128)(2,1)S(1)}, bf16[2,512,2,128]{3,2,1,0:T(2,128)(2,1)}, u32[]{:S(2)}) copy-start(bf16[2,512,2,128]{3,2,1,0:T(2,128)(2,1)} %get-tuple-element.141) | copy-start | bytes 1572868 | tf_op jit(solution)/shard_map/while
  195.5 0.8 copy-start.2
  204.8 3.0 %copy-start.1 = (bf16[2,512,2,128]{3,2,1,0:T(2,128)(2,1)S(1)}, bf16[2,512,2,128]{3,2,1,0:T(2,128)(2,1)}, u32[]{:S(2)}) copy-start(bf16[2,512,2,128]{3,2,1,0:T(2,128)(2,1)} %get-tuple-element.141) | copy-start | bytes 1572868 | tf_op jit(solution)/shard_map/while
  208.2 0.8 copy-start.2
Sparse Core Ops, SparseCore 0:
  9.0 135.1 all-gather.1
  213.4 68.7 reduce-scatter.1

commit v2 on v1

--- a/solution.py
+++ b/solution.py
@@ -3,7 +3,7 @@
 import jax
 import jax.numpy as jnp
 from jax import lax
-from jax.sharding import PartitionSpec as P
+from jax.sharding import Mesh, PartitionSpec as P
 
 HEADS = 32
 HS = 128
@@ -62,24 +62,25 @@
     adapter_up,
     lengths,
 ):
-    col_count = lax.axis_size("col")
-    whole = lax.all_gather(inputs, "col", axis=1, tiled=True)
+    row_count = lax.axis_size("row")
+    col_count = lax.axis_size("chip") * lax.axis_size("core")
+    tok_count = inputs.shape[0]
+    part = lax.all_gather(inputs, "chip", axis=1, tiled=False)
+    whole = lax.all_gather(part, "core", axis=2, tiled=False).reshape(tok_count, -1)
     normed = normalize(whole, norm_gain)
-    tok_count = normed.shape[0]
     adapted = jnp.dot(normed, adapter_down, preferred_element_type=jnp.float32).astype(jnp.bfloat16)
     local_rows = query_train.shape[0]
-    row_count = lax.axis_size("row")
     head_local = HEADS // col_count
     merged_width = 3 * head_local * HS
     trained = jnp.stack(
         (query_train.astype(jnp.bfloat16), key_train.astype(jnp.bfloat16), value_train.astype(jnp.bfloat16)),
         axis=1,
     ).reshape(local_rows, 3, col_count, head_local * HS)
-    trained = jnp.transpose(trained, (2, 0, 1, 3)).reshape(col_count, local_rows, merged_width)
-    sent = jnp.broadcast_to(trained[None], (row_count,) + trained.shape).reshape(
-        row_count * col_count, local_rows, merged_width
-    )
-    merged = lax.all_to_all(sent, ("row", "col"), 0, 0, tiled=True).reshape(-1, merged_width)
+    trained = jnp.transpose(trained, (2, 0, 1, 3))
+    moved = lax.all_to_all(trained, ("chip", "core"), 0, 0, tiled=True)
+    moved = moved.reshape(col_count * local_rows, merged_width)
+    sent = jnp.broadcast_to(moved[None], (row_count,) + moved.shape)
+    merged = lax.all_to_all(sent, "row", 0, 0, tiled=True).reshape(-1, merged_width)
     product = jnp.dot(normed, merged, preferred_element_type=jnp.float32)
     up_columns = adapter_up.reshape(adapter_up.shape[0], merged_width)
     joined = (product + jnp.dot(adapted, up_columns, preferred_element_type=jnp.float32)).astype(
@@ -90,32 +91,35 @@
     attended = attend(joined[:, 0], joined[:, 1], joined[:, 2], segment)
     out_local = out_train.astype(jnp.bfloat16)
     out_cols = out_local.shape[1]
-    out_sent = out_local.reshape(col_count, head_local * HS, out_cols)
-    out_sent = jnp.broadcast_to(out_sent[None], (row_count,) + out_sent.shape).reshape(
-        row_count * col_count, head_local * HS, out_cols
+    out_moved = lax.all_to_all(
+        out_local.reshape(col_count, head_local * HS, out_cols), ("chip", "core"), 0, 0, tiled=True
     )
-    out_block = lax.all_to_all(out_sent, ("row", "col"), 0, 0, tiled=True)
-    out_block = jnp.transpose(out_block, (1, 0, 2)).reshape(head_local * HS, -1)
+    out_sent = jnp.broadcast_to(out_moved[None], (row_count,) + out_moved.shape)
+    out_block = lax.all_to_all(out_sent, "row", 0, 0, tiled=True)
+    out_block = jnp.transpose(out_block, (2, 0, 1, 3)).reshape(head_local * HS, -1)
     partial_out = jnp.dot(attended, out_block, preferred_element_type=jnp.float32)
     mixed = lax.psum_scatter(
-        partial_out.astype(jnp.bfloat16), "col", scatter_dimension=0, tiled=True
+        partial_out.astype(jnp.bfloat16), ("chip", "core"), scatter_dimension=0, tiled=True
     )
     return mixed
 
 
 def solution(mesh):
+    row_count, col_count = mesh.devices.shape
+    split = Mesh(mesh.devices.reshape(row_count, col_count // 2, 2), ("row", "chip", "core"))
+    col = ("chip", "core")
     in_specs = (
-        P("row", "col"),
+        P("row", col),
         P(),
-        P(("row", "col"), None),
-        P(("row", "col"), None),
-        P(("row", "col"), None),
-        P(None, ("row", "col")),
+        P(("row",) + col, None),
+        P(("row",) + col, None),
+        P(("row",) + col, None),
+        P(None, ("row",) + col),
         P(),
-        P(None, None, "col", None),
+        P(None, None, col, None),
         P("row", None),
     )
-    out_specs = P(("row", "col"), None)
+    out_specs = P(("row",) + col, None)
     return jax.shard_map(
-        on_device, mesh=mesh, in_specs=in_specs, out_specs=out_specs, check_vma=False
+        on_device, mesh=split, in_specs=in_specs, out_specs=out_specs, check_vma=False
     )

time: 290 us -> 344 us (1.19)
  waiting for transfers between devices: 184 us -> 228 us
  other arithmetic: 11.8 us -> 20.1 us
  matrix products: 41.4 us -> 37.9 us
    all_to_all x2 -> x4, waiting for transfers between devices: 0.01 us -> 96 us  [the longest x1 77.2 us: on_device(): lax.all_to_all(sent, 'row', 0, 0, tiled=True).reshape(-1, merged_width)]
    all_gather x1 -> x2, waiting for transfers between devices: 115 us -> 64 us  [the longest x1 64 us: on_device(): part = lax.all_gather(inputs, 'chip', axis=1, tiled=False)]
    convert_element_type x0 -> x2, other arithmetic: none -> 12 us  [normalize(): (floats * lax.rsqrt(mean_square + 1e-05) * norm_gain).astype(jnp.bfloat16)]
    all_gather x0 -> x1, local copies, waits for them, and re-layouts: none -> 6.3 us  [on_device(): part = lax.all_gather(inputs, 'chip', axis=1, tiled=False)]
    all_to_all x2 -> x4, starting transfers between devices: 17.3 us -> 20.4 us  [the longest x1 6.81 us: on_device(): lax.all_to_all(sent, 'row', 0, 0, tiled=True).reshape(-1, merged_width)]
  transfers between devices with their start and end apart: 4 -> 7, of which waited for: 2 -> 5; matrix products, arithmetic and copies ran while one was open for 22% -> 18% of each run, Pallas kernels for 0% -> 0%
where the time goes in v2:
time: 344 us; the launch traced here: 343 us
  waiting for transfers between devices  228 us (66%)
  matrix products  37.9 us (11%)
  starting transfers between devices  20.6 us (6%)
  other arithmetic  20.1 us (6%)
  local copies, waits for them, and re-layouts  18.6 us (5%)
  between operations  13.4 us (4%)
  loops' own time  3.85 us (1%)
    all_to_all x1, waiting for transfers between devices, on_device(): lax.all_to_all(sent, 'row', 0, 0, tiled=True).reshape(-1, merged_width)  77.2 us
    reduce_scatter x1, waiting for transfers between devices, on_device(): lax.psum_scatter(partial_out.astype(jnp.bfloat16), ('chip', 'core'), scat...  67.6 us
    all_gather x1, waiting for transfers between devices, on_device(): part = lax.all_gather(inputs, 'chip', axis=1, tiled=False)  64 us
    all_to_all x1, waiting for transfers between devices, on_device(): moved = lax.all_to_all(trained, ('chip', 'core'), 0, 0, tiled=True)  13 us
    dot_general x1, matrix products, on_device(): product = jnp.dot(normed, merged, preferred_element_type=jnp.float32)  12.2 us
    convert_element_type x2, other arithmetic, normalize(): (floats * lax.rsqrt(mean_square + 1e-05) * norm_gain).astype(jnp.bfloat16)  12 us
    dot_general x1, matrix products, on_device(): jnp.dot(adapted, up_columns, preferred_element_type=jnp.float32)  7.75 us
    sub x2, matrix products, one_block(): exponent = jnp.exp(scores - highest)  7.26 us
  transfers between devices with their start and end apart: 7, of which 5 were waited for; matrix products, arithmetic and copies ran while one was open for 18% of the time, Pallas kernels for 0%

profile of v2, /device:TPU:0, one launch (start us, length us, event | category | flops | bytes accessed | tf_op | source)
XLA Modules:
  0.0 342.8 jit_solution(17338425987214270672)
XLA Ops:
  6.5 0.7 all-gather.5.cloned.1.call-update
  7.3 64.0 %all-gather.5.cloned.1.call-done = bf16[1024,2048]{1,0:T(8,128)(2,1)} async-done(((bf16[1024,256]{1,0:T(8,128)(2,1)}), bf16[1024,2048]{1,0:T(8,128)(2,1)}) %all-gather.5.cloned.1.call-update) | async-done | bytes 4194320 | tf_op jit(solution)/shard_map/all_gather | solution.py:68
  71.4 6.3 %copy.46 = bf16[1024,2048]{0,1:T(8,128)(2,1)} copy(bf16[1024,2048]{1,0:T(8,128)(2,1)} %all-gather.5.cloned.1.call-done) | data formatting | bytes 8388608 | tf_op jit(solution)/shard_map/all_gather | solution.py:68
  78.0 0.1 maximum_bitcast_fusion
  78.1 1.2 copy.39
  79.3 5.0 %all-to-all-start = ((bf16[16,32,3,256]{3,1,2,0:T(8,128)(2,1)}), bf16[16,32,3,256]{3,1,2,0:T(8,128)(2,1)S(1)}, u32[]{:S(2)}, u32[]{:S(2)}) async-start(bf16[16,32,3,256]{3,1,2,0:T(8,128)(2,1)} %copy.39), calls=%async_computation | async-start | bytes 1572864 | tf_op jit(solution)/shard_map/all_to_all | solution.py:80
  84.3 0.7 copy.64
  85.0 13.0 %all-to-all-done = bf16[16,32,3,256]{3,1,2,0:T(8,128)(2,1)S(1)} async-done(((bf16[16,32,3,256]{3,1,2,0:T(8,128)(2,1)}), bf16[16,32,3,256]{3,1,2,0:T(8,128)(2,1)S(1)}, u32[]{:S(2)}, u32[]{:S(2)}) %all-to-all-start) | async-done | bytes 786464 | tf_op jit(solution)/shard_map/all_to_all | solution.py:80
  98.0 3.5 %all-to-all-start.2 = ((bf16[16,256,16]{1,2,0:T(8,128)(2,1)}), bf16[16,256,16]{1,2,0:T(8,128)(2,1)S(1)}, u32[]{:S(2)}, u32[]{:S(2)}) async-start(bf16[16,256,16]{1,2,0:T(8,128)(2,1)} %bitcast.60), calls=%async_computation.2 | async-start | bytes 262144 | tf_op jit(solution)/shard_map/all_to_all | solution.py:94
  101.5 0.7 copy.40
  102.2 0.2 copy.56
  102.4 5.8 %all-to-all-done.2 = bf16[16,256,16]{1,2,0:T(8,128)(2,1)S(1)} async-done(((bf16[16,256,16]{1,2,0:T(8,128)(2,1)}), bf16[16,256,16]{1,2,0:T(8,128)(2,1)S(1)}, u32[]{:S(2)}, u32[]{:S(2)}) %all-to-all-start.2) | async-done | bytes 131104 | tf_op jit(solution)/shard_map/all_to_all | solution.py:94
  108.2 3.1 broadcast_in_dim.33
  111.2 6.8 %all-to-all-start.1 = ((bf16[8,512,768]{2,1,0:T(8,128)(2,1)}), bf16[8,512,768]{2,1,0:T(8,128)(2,1)}, u32[]{:S(2)}, u32[]{:S(2)}) async-start(bf16[8,512,768]{2,1,0:T(8,128)(2,1)} %broadcast_in_dim.33), calls=%async_computation.1 | async-start | bytes 12582912 | tf_op jit(solution)/shard_map/all_to_all | solution.py:83
  118.1 0.1 reshape.139
  118.2 0.2 reduce-window.8
  118.4 0.1 convert_reduce_fusion
  118.5 5.2 %multiply_reduce_fusion = f32[1024]{0:T(1024)S(1)} fusion(bf16[1024,8,2,256]{0,3,2,1:T(8,128)(2,1)} %bitcast.69), kind=kLoop, calls=%fused_computation.28 | loop fusion | flops 12581888 | bytes 8392704 | tf_op jit(solution)/shard_map/reduce_sum | solution.py:14
  123.7 0.5 copy-done.2
  124.3 4.3 %multiply_convert_fusion = bf16[1024,8,2,256]{0,3,2,1:T(8,128)(2,1)} fusion(f32[8,2,256]{2,1,0:T(2,128)S(1)} %mul.42, f32[1024]{0:T(1024)S(1)} %add_rsqrt_fusion, bf16[1024,8,512]{0,2,1:T(8,128)(2,1)S(1)} %copy-done.2), kind=kLoop, calls=%fused_computation.27 | loop fusion | flops 16777216 | bytes 16797696 | tf_op jit(solution)/shard_map/convert_element_type | solution.py:15
  128.6 77.2 %all-to-all-done.1 = bf16[8,512,768]{2,1,0:T(8,128)(2,1)} async-done(((bf16[8,512,768]{2,1,0:T(8,128)(2,1)}), bf16[8,512,768]{2,1,0:T(8,128)(2,1)}, u32[]{:S(2)}, u32[]{:S(2)}) %all-to-all-start.1) | async-done | bytes 6291488 | tf_op jit(solution)/shard_map/all_to_all | solution.py:83
  205.7 1.1 broadcast_in_dim.34
  206.8 5.1 %all-to-all-start.3 = ((bf16[8,16,256,16]{2,3,1,0:T(8,128)(2,1)}), bf16[8,16,256,16]{2,3,1,0:T(8,128)(2,1)}, u32[]{:S(2)}, u32[]{:S(2)}) async-start(bf16[8,16,256,16]{2,3,1,0:T(8,128)(2,1)} %broadcast_in_dim.34), calls=%async_computation.3 | async-start | bytes 2097152 | tf_op jit(solution)/shard_map/all_to_all | solution.py:98
  211.9 0.2 reduce-scatter.2.cloned.1.call-start
  212.1 12.2 %fusion.36 = f32[1024,768]{0,1:T(8,128)} fusion(bf16[1024,4096]{0,1:T(8,128)(2,1)} %bitcast.71, bf16[4096,768]{1,0:T(8,128)(2,1)} %bitcast.6), kind=kOutput, calls=%fused_computation.42 | convolution fusion | flops 6442450944 | bytes 17825792 | tf_op jit(solution)/shard_map/dot_general | solution.py:84
  224.3 7.7 %fusion.27 = bf16[1024,4096]{0,1:T(8,128)(2,1)} fusion(f32[4096]{0:T(1024)S(1)} %copy-done.10, f32[1024]{0:T(1024)S(1)} %add_rsqrt_fusion, bf16[1024,8,512]{0,2,1:T(8,128)(2,1)} %all-gather.7.cloned.1.call-done), kind=kLoop, calls=%fused_computation.26 | loop fusion | flops 16777216 | bytes 16797696 | tf_op jit(solution)/shard_map/convert_element_type | solution.py:15
  232.0 7.7 %add_convert_fusion = bf16[1024,768]{0,1:T(8,128)(2,1)S(1)} fusion(f32[1024,768]{0,1:T(8,128)} %fusion.36, bf16[128,768]{1,0:T(8,128)(2,1)S(1)} %reshape.139, bf16[1024,4096]{0,1:T(8,128)(2,1)} %fusion.27, bf16[4096,128]{1,0:T(8,128)(2,1)S(1)} %copy-done), kind=kOutput, calls=%fused_computation.30 | convolution fusion | flops 1276772352 | bytes 14352384 | tf_op jit(solution)/shard_map/dot_general | solution.py:86
  239.7 0.2 fusion.35
  239.9 0.3 copy.50
  240.2 0.3 copy.51
  240.5 0.3 copy.49
  240.7 23.2 %while.11 = (s32[]{:T(128)}, bf16[2,512,2,128]{3,2,1,0:T(2,128)(2,1)}, s32[2]{0:T(128)S(1)}, s32[1024]{0:T(1024)S(1)}, bf16[1024,2,128]{2,0,1:T(8,128)(2,1)S(1)}...) while((s32[]{:T(128)}, ...), condition=%wide.region_6.7_spmd.clone, body=%wide.region_3.6_spmd.clone.sunk | while | flops 544867840 | bytes 15751387 | solution.py:50
  240.8 0.7 dynamic_slice.29
  243.4 0.6 iota_add_fusion.2
  244.0 0.6 fusion.55
  244.6 3.6 %fusion.56 = (f32[2,512]{1,0:T(2,128)S(1)}, f32[2,512,1024]{2,1,0:T(8,128)}) fusion(pred[512,1024]{1,0:T(8,128)(4,1)S(1)} %fusion.55, bf16[1024,2,128]{2,0,1:T(8,128)(2,1)S(1)} %get-tuple-element.155, bf16[1024,2,128]{2,0,1:T(8,128)(2,1)S(1)} %get-tuple-element.154, s32[]{:T(128)S(6)} %select_n.23), kind=kOutput, calls=%fused_computation.40.clone.1 | convolution fusion | flops 272630784 | bytes 5509124 | tf_op jit(solution)/shard_map/while/body/eval_jaxpr/sub | solution.py:43
  248.2 3.0 fusion.57
  251.2 0.3 copy_dynamic-update-slice_fusion.2
  251.5 0.8 copy-done.4
  252.3 0.6 dynamic_slice.29
  254.9 0.6 iota_add_fusion.2
  255.6 0.6 fusion.55
  256.1 3.6 %fusion.56 = (f32[2,512]{1,0:T(2,128)S(1)}, f32[2,512,1024]{2,1,0:T(8,128)}) fusion(pred[512,1024]{1,0:T(8,128)(4,1)S(1)} %fusion.55, bf16[1024,2,128]{2,0,1:T(8,128)(2,1)S(1)} %get-tuple-element.155, bf16[1024,2,128]{2,0,1:T(8,128)(2,1)S(1)} %get-tuple-element.154, s32[]{:T(128)S(6)} %select_n.23), kind=kOutput, calls=%fused_computation.40.clone.1 | convolution fusion | flops 272630784 | bytes 5509124 | tf_op jit(solution)/shard_map/while/body/eval_jaxpr/sub | solution.py:43
  259.8 3.0 fusion.57
  262.8 0.3 copy_dynamic-update-slice_fusion.2
  263.1 0.8 copy-done.4
  263.9 4.7 %convolution_convert_fusion = bf16[1024,2048]{1,0:T(8,128)(2,1)} fusion(bf16[256,2048]{0,1:T(8,128)(2,1)} %bitcast.13, bf16[128,8,2,128]{3,2,1,0:T(2,128)(2,1)} %bitcast.75), kind=kOutput, calls=%fused_computation.29 | convolution fusion | flops 1075838976 | bytes 5767168 | tf_op jit(solution)/shard_map/dot_general | solution.py:100
  268.7 67.6 %reduce-scatter.2.cloned.1.call-done = bf16[64,2048]{1,0:T(8,128)(2,1)} async-done(((bf16[1024,2048]{1,0:T(8,128)(2,1)}), bf16[64,2048]{1,0:T(8,128)(2,1)}) %reduce-scatter.2.cloned.1.call-update) | async-done | bytes 262160 | tf_op jit(solution)/shard_map/reduce_scatter | solution.py:101
  (44 shorter events, 0.6 us)
Async XLA Ops:
  6.5 225.5 %copy-start = (bf16[4096,128]{1,0:T(8,128)(2,1)S(1)}, bf16[4096,128]{1,0:T(8,128)(2,1)}, u32[]{:S(2)}) copy-start(bf16[4096,128]{1,0:T(8,128)(2,1)} %param.17) | copy-start | bytes 3145732
  6.5 64.8 %all-gather.5.cloned.1.call-start = ((), (), s32[]{:S(2)}) async-start(), calls=%async_computation.6 | async-start | bytes 4718592 | tf_op jit(solution)/shard_map/all_gather | solution.py:68
  7.3 70.4 %copy-start.5 = (f32[32,4096]{1,0:T(8,128)S(1)}, f32[32,4096]{1,0:T(8,128)}, u32[]{:S(2)}) copy-start(f32[32,4096]{1,0:T(8,128)} %param.13) | copy-start | bytes 1572868
  7.3 70.5 %copy-start.6 = (f32[32,4096]{1,0:T(8,128)S(1)}, f32[32,4096]{1,0:T(8,128)}, u32[]{:S(2)}) copy-start(f32[32,4096]{1,0:T(8,128)} %param.14) | copy-start | bytes 1572868
  7.3 70.6 %copy-start.7 = (f32[32,4096]{1,0:T(8,128)S(1)}, f32[32,4096]{1,0:T(8,128)}, u32[]{:S(2)}) copy-start(f32[32,4096]{1,0:T(8,128)} %param.15) | copy-start | bytes 1572868
  7.3 111.2 %all-gather.7.cloned.1.call-start = ((), (), s32[]{:S(2)}) async-start(), calls=%async_computation.7 | async-start | bytes 12582912 | tf_op jit(solution)/shard_map/all_gather | solution.py:69
  77.7 6.6 %copy-start.8 = (f32[4096,16]{0,1:T(8,128)S(1)}, f32[4096,16]{0,1:T(8,128)}, u32[]{:S(2)}) copy-start(f32[4096,16]{0,1:T(8,128)} %param.16) | copy-start | bytes 786436
  79.3 18.7 %all-to-all-start = ((bf16[16,32,3,256]{3,1,2,0:T(8,128)(2,1)}), bf16[16,32,3,256]{3,1,2,0:T(8,128)(2,1)S(1)}, u32[]{:S(2)}, u32[]{:S(2)}) async-start(bf16[16,32,3,256]{3,1,2,0:T(8,128)(2,1)} %copy.39), calls=%async_computation | async-start | bytes 1572864 | tf_op jit(solution)/shard_map/all_to_all | solution.py:80
  98.0 10.2 %all-to-all-start.2 = ((bf16[16,256,16]{1,2,0:T(8,128)(2,1)}), bf16[16,256,16]{1,2,0:T(8,128)(2,1)S(1)}, u32[]{:S(2)}, u32[]{:S(2)}) async-start(bf16[16,256,16]{1,2,0:T(8,128)(2,1)} %bitcast.60), calls=%async_computation.2 | async-start | bytes 262144 | tf_op jit(solution)/shard_map/all_to_all | solution.py:94
  111.2 6.8 %copy-start.10 = (f32[4096]{0:T(1024)S(1)}, f32[4096]{0:T(1024)}, u32[]{:S(2)}) copy-start(f32[4096]{0:T(1024)} %param.12) | copy-start | bytes 49156
  111.2 6.8 %copy-start.9 = (bf16[128,3,2,128]{3,2,1,0:T(2,128)(2,1)S(1)}, bf16[128,3,2,128]{3,2,1,0:T(2,128)(2,1)}, u32[]{:S(2)}) copy-start(bf16[128,3,2,128]{3,2,1,0:T(2,128)(2,1)} %param.18) | copy-start | bytes 589828
  111.2 7.0 %copy-start.11 = (s32[1,7]{1,0:T(1,128)S(1)}, s32[1,7]{1,0:T(1,128)}, u32[]{:S(2)}) copy-start(s32[1,7]{1,0:T(1,128)} %param.19) | copy-start | bytes 88
  111.2 94.5 %all-to-all-start.1 = ((bf16[8,512,768]{2,1,0:T(8,128)(2,1)}), bf16[8,512,768]{2,1,0:T(8,128)(2,1)}, u32[]{:S(2)}, u32[]{:S(2)}) async-start(bf16[8,512,768]{2,1,0:T(8,128)(2,1)} %broadcast_in_dim.33), calls=%async_computation.1 | async-start | bytes 12582912 | tf_op jit(solution)/shard_map/all_to_all | solution.py:83
  118.5 5.8 %copy-start.2 = (bf16[1024,8,512]{0,2,1:T(8,128)(2,1)S(1)}, bf16[1024,8,512]{0,2,1:T(8,128)(2,1)}, u32[]{:S(2)}) copy-start(bf16[1024,8,512]{0,2,1:T(8,128)(2,1)} %all-gather.7.cloned.1.call-done) | copy-start | bytes 25165828
  206.8 57.1 %all-to-all-start.3 = ((bf16[8,16,256,16]{2,3,1,0:T(8,128)(2,1)}), bf16[8,16,256,16]{2,3,1,0:T(8,128)(2,1)}, u32[]{:S(2)}, u32[]{:S(2)}) async-start(bf16[8,16,256,16]{2,3,1,0:T(8,128)(2,1)} %broadcast_in_dim.34), calls=%async_computation.3 | async-start | bytes 2097152 | tf_op jit(solution)/shard_map/all_to_all | solution.py:98
  211.9 124.3 %reduce-scatter.2.cloned.1.call-start = ((), (), s32[]{:S(2)}) async-start(), calls=%async_computation.5 | async-start | bytes 4456448 | tf_op jit(solution)/shard_map/reduce_scatter | solution.py:101
  248.2 3.0 copy-start.3
  251.5 0.8 copy-start.4
  259.8 3.0 copy-start.3
  263.1 0.8 copy-start.4
  263.9 72.3 %copy-start.1 = (bf16[4096,128]{1,0:T(8,128)(2,1)S(1)}, bf16[4096,128]{1,0:T(8,128)(2,1)}, u32[]{:S(2)}) copy-start(bf16[4096,128]{1,0:T(8,128)(2,1)} %param.17) | copy-start | bytes 3145732
Sparse Core Ops, SparseCore 0:
  8.9 62.4 all-gather.4
  77.8 23.9 all-gather.6
  268.8 67.4 reduce-scatter.1
